TPU v7x, 32 devices: a whole 2x2x4 slice. The times are simulated.
32 devices in a mesh: pair: 8 (over z, y), virt: 4 (over x, core).
Axes of the slice: x: 2, y: 2, z: 4, core: 2. Of those that a mesh axis runs over, the one named last changes fastest.
Arguments:
- amps_pm: bfloat16 [64, 64, 4096], P(('pair', 'virt')), may hold values from -6 to 6
- integrals: bfloat16 [32, 4096, 2048], P(('pair', 'virt')), may hold values from -0.046875 to 0.046875
- fock_vv: bfloat16 [512, 512], replicated, may hold values from -0.25 to 0.25
- blk_tiles: int32 [32, 2], replicated, may hold values from 0 to 63, as said below
- blk_mask: int32 [32], replicated, may hold values 0 or 1
Outputs:
- sigma: bfloat16 [64, 64, 2048], P('pair', 'virt')
Inputs may be any that keep to these rules, and one draw needn't show every extreme that they name: Each row is (input tile pair, output tile pair). Integral tile r belongs to device r // 1 of the joined axis pair+virt, and its input tile pair lies in that device's virt slab: blk_tiles[r, 0] // 16 == (r) % 4. No two rows are equal.
All inputs are finite; a program needn't handle non-finite values.
Results may differ from a plain program's by a relative error of at most 0.0033.
Values may be sent and summed in bfloat16 or wider, within the bound.
No kernel may reach another device: no remote copies, remote signals or barrier semaphores. Data moves between devices by JAX's collectives and lax.ppermute only.
A program may use at most 128 MiB of HBM per device.

v0:
```python
import jax
import jax.numpy as jnp
from jax import lax
from jax.sharding import PartitionSpec as P

TILE = 64
NVT = 8
AS = 32


def per_device(amps_pm, integrals, fock_vv, blk_tiles, blk_mask):
    n_virt = lax.axis_size("virt")
    n_pair = lax.axis_size("pair")
    n_dev = n_virt * n_pair
    pm_rows, n_tiles, tile_len = amps_pm.shape
    out_cols = integrals.shape[2]
    slab = n_tiles // n_virt
    device = lax.axis_index(("pair", "virt"))
    virt_idx = lax.axis_index("virt")
    p_grp = pm_rows * n_virt
    tin_all = blk_tiles[:, 0]
    picked = jnp.take(amps_pm, tin_all, axis=1)
    picked = jnp.transpose(picked, (1, 0, 2))
    chosen = lax.all_to_all(picked, ("pair", "virt"), 0, 0, tiled=True)
    chosen = chosen.reshape(n_dev * pm_rows, tile_len)
    sub = lax.all_to_all(amps_pm[:, :, :out_cols], "virt", split_axis=1, concat_axis=0, tiled=True)
    sub = sub.reshape(p_grp, slab // NVT, NVT, AS, TILE)
    fock_four = fock_vv.reshape(NVT, TILE, NVT, TILE)
    onebody = jnp.einsum(
        "pkqsd,bjqd->pkbsj", sub, fock_four, preferred_element_type=jnp.float32
    ).reshape(p_grp, slab, out_cols)
    own_tiles = lax.dynamic_index_in_dim(blk_tiles, device, 0, keepdims=False)
    own_mask = lax.dynamic_index_in_dim(blk_mask, device, 0, keepdims=False)
    product = jnp.dot(chosen, integrals[0], preferred_element_type=jnp.float32)
    product = (product * own_mask.astype(jnp.float32)).astype(jnp.bfloat16)
    dest_virt = own_tiles[1] // slab
    select = (jnp.arange(n_virt, dtype=jnp.int32) == dest_virt).astype(jnp.bfloat16)
    outgoing = product.reshape(n_pair, 1, p_grp, out_cols) * select[None, :, None, None]
    outgoing = outgoing.reshape(n_dev, p_grp, out_cols)
    received = lax.all_to_all(outgoing, ("pair", "virt"), 0, 0, tiled=True)
    my_tiles = virt_idx * slab + jnp.arange(slab, dtype=jnp.int32)
    one_hot = (blk_tiles[:, 1][:, None] == my_tiles[None, :]).astype(jnp.bfloat16)
    ladder = jnp.einsum("rpo,rt->pto", received, one_hot, preferred_element_type=jnp.float32)
    return (ladder + onebody).astype(jnp.bfloat16)


def solution(mesh):
    return jax.shard_map(
        per_device,
        mesh=mesh,
        in_specs=(P(("pair", "virt"), None, None), P(("pair", "virt"), None, None), P(), P(), P()),
        out_specs=P("pair", "virt", None),
        check_vma=False,
    )
```

profile of v0, /device:TPU:0, one launch (start us, length us, event | category | flops | bytes accessed | tf_op | source)
XLA Modules:
  0.0 75.2 jit_solution(7322697430825926333)
XLA Ops:
  0.0 0.8 %slice_bitcast_fusion = (s32[32]{0:T(128)S(1)}, s32[32]{0:T(128)S(1)}) fusion(s32[32,2]{0,1:T(2,128)} %param.8), kind=kLoop, calls=%fused_computation.24 | loop fusion | flops 96 | bytes 512 | tf_op jit(solution)/shard_map/eq | solution.py:42
  0.8 0.7 and_bitcast_fusion
  1.5 2.6 %gather_fusion = bf16[32,2,4096]{2,0,1:T(8,128)(2,1)S(1)} fusion(bf16[2,64,4096]{2,1,0:T(8,128)(2,1)} %param.5, s32[1024]{0:T(1024)S(1)} %pad_clamp_fusion), kind=kCustom, calls=%fused_computation | custom fusion | bytes 1048704 | tf_op jit(solution)/shard_map/jit(_take)/gather | solution.py:22
  4.0 0.1 broadcast_select_fusion
  4.2 1.3 %copy.15 = bf16[32,2,4096]{2,1,0:T(2,128)(2,1)} copy(bf16[32,2,4096]{2,0,1:T(8,128)(2,1)S(1)} %broadcast_select_fusion) | data formatting | bytes 1048576 | tf_op jit(solution)/shard_map/jit(_take)/select_n | solution.py:22
  5.5 0.0 copy-start
  5.5 7.3 %all-to-all-start = ((bf16[32,2,4096]{2,1,0:T(2,128)(2,1)}), bf16[32,2,4096]{2,1,0:T(2,128)(2,1)S(1)}, u32[]{:S(2)}, u32[]{:S(2)}) async-start(bf16[32,2,4096]{2,1,0:T(2,128)(2,1)} %copy.15), calls=%async_computation | async-start | bytes 1048576 | tf_op jit(solution)/shard_map/all_to_all | solution.py:24
  12.8 1.1 %slice.16 = bf16[2,64,2048]{2,1,0:T(8,128)(2,1)S(1)} slice(bf16[2,64,4096]{2,1,0:T(8,128)(2,1)} %param.5), slice={[0:2], [0:64], [0:2048]} | slice | bytes 1048576 | tf_op jit(solution)/shard_map/slice | solution.py:26
  13.9 0.8 %constant_dynamic-slice_fusion = s32[1,2]{0,1:T(2,128)S(1)} fusion(s32[32,2]{0,1:T(2,128)} %param.8, s32[]{:T(128)S(6)} %select_n.29), kind=kLoop, calls=%fused_computation.25 | loop fusion | bytes 20 | tf_op jit(solution)/shard_map/jit(dynamic_index_in_dim)/dynamic_slice | solution.py:32
  14.7 0.5 slice.15
  17.1 1.3 %copy.25 = bf16[2,64,2048]{2,0,1:T(2,128)(2,1)} copy(bf16[2,64,2048]{2,1,0:T(8,128)(2,1)S(1)} %slice.16) | data formatting | bytes 1048576
  19.1 0.1 mul.42
  19.2 1.3 %dynamic_slice.8 = s32[1]{0:T(128)} dynamic-slice(s32[32]{0:T(128)} %param.9, s32[]{:T(128)S(6)} %select_n.29), dynamic_slice_sizes={1} | dynamic-slice | bytes 12 | tf_op jit(solution)/shard_map/jit(dynamic_index_in_dim)/dynamic_slice | solution.py:33
  21.1 7.4 %all-to-all-done = bf16[32,2,4096]{2,1,0:T(2,128)(2,1)S(1)} async-done(((bf16[32,2,4096]{2,1,0:T(2,128)(2,1)}), bf16[32,2,4096]{2,1,0:T(2,128)(2,1)S(1)}, u32[]{:S(2)}, u32[]{:S(2)}) %all-to-all-start) | async-done | bytes 524320 | tf_op jit(solution)/shard_map/all_to_all | solution.py:24
  28.4 3.5 %all-to-all-start.2 = ((bf16[2,64,2048]{2,0,1:T(2,128)(2,1)}), bf16[2,64,2048]{2,0,1:T(2,128)(2,1)S(1)}, u32[]{:S(2)}, u32[]{:S(2)}) async-start(bf16[2,64,2048]{2,0,1:T(2,128)(2,1)} %copy.25), calls=%async_computation.2 | async-start | bytes 1048576 | tf_op jit(solution)/shard_map/all_to_all | solution.py:26
  31.9 0.2 reshape.34
  32.1 8.8 %fusion.10 = bf16[8,8,2048]{2,1,0:T(8,128)(2,1)S(1)} fusion(bf16[64,4096]{1,0:T(8,128)(2,1)S(1)} %reshape.34, bf16[1,4096,2048]{2,1,0:T(8,128)(2,1)} %param.6, f32[]{:T(128)} %bitcast.5), kind=kOutput, calls=%fused_computation.8 | convolution fusion | flops 1074003968 | bytes 17563652 | tf_op jit(solution)/shard_map/dot_general | solution.py:34
  40.9 1.2 %bitcast_multiply_fusion = bf16[32,8,2048]{2,1,0:T(8,128)(2,1)} fusion(bf16[32]{0:T(256)(128)(2,1)S(1)} %mul.42, bf16[8,8,2048]{2,1,0:T(8,128)(2,1)S(1)} %fusion.10), kind=kLoop, calls=%fused_computation.11 | loop fusion | flops 524288 | bytes 1310784 | tf_op jit(solution)/shard_map/mul | solution.py:38
  42.1 0.0 all-to-all-done.2
  42.1 3.6 %all-to-all-start.1 = ((bf16[32,8,2048]{2,1,0:T(8,128)(2,1)}), bf16[32,8,2048]{2,1,0:T(8,128)(2,1)}, u32[]{:S(2)}, u32[]{:S(2)}) async-start(bf16[32,8,2048]{2,1,0:T(8,128)(2,1)} %bitcast_multiply_fusion), calls=%async_computation.1 | async-start | bytes 2097152 | tf_op jit(solution)/shard_map/all_to_all | solution.py:40
  45.7 0.0 copy-done
  45.8 0.5 reshape.35
  46.3 0.2 copy.31
  46.5 1.1 %reshape.48 = bf16[8,2,8,32,64,1]{4,3,2,1,0,5:T(8,128)(2,1)S(1)} reshape(bf16[4,2,16,2048]{3,2,1,0:T(8,128)(2,1)S(1)} %bitcast.46) | data formatting | bytes 1048576 | tf_op jit(solution)/shard_map/reshape | solution.py:27
  47.5 1.3 %convolution_bitcast_fusion.1 = f32[8,2,8,32,64]{4,3,1,0,2:T(8,128)S(1)} fusion(bf16[8,2,8,32,64,1]{4,3,2,1,0,5:T(8,128)(2,1)S(1)} %reshape.48, bf16[8,64,8,64,1,1]{3,2,1,0,5,4:T(8,128)(2,1)S(1)} %bitcast.48), kind=kOutput, calls=%fused_computation.9 | convolution fusion | flops 268435456 | bytes 2097152 | tf_op jit(solution)/shard_map/pkqsd,bjqd->pkbsj/dot_general | solution.py:29
  48.8 0.2 copy.20
  49.0 0.7 reshape.37
  49.7 22.2 %all-to-all-done.1 = bf16[32,8,2048]{2,1,0:T(8,128)(2,1)} async-done(((bf16[32,8,2048]{2,1,0:T(8,128)(2,1)}), bf16[32,8,2048]{2,1,0:T(8,128)(2,1)}, u32[]{:S(2)}, u32[]{:S(2)}) %all-to-all-start.1) | async-done | bytes 1048608 | tf_op jit(solution)/shard_map/all_to_all | solution.py:40
  71.9 3.2 %fusion.3 = bf16[8,16,2048]{2,1,0:T(8,128)(2,1)} fusion(f32[8,16,2048]{2,1,0:T(8,128)S(1)} %reshape.37, bf16[32,8,2048]{2,1,0:T(8,128)(2,1)} %all-to-all-done.1, s32[32]{0:T(128)S(1)} %get-tuple-element.5, s32[16]{0:T(128)S(1)} %iota_add_fusion), kind=kOutput, calls=%fused_computation.5 | convolution fusion | flops 17302016 | bytes 2621632 | tf_op jit(solution)/shard_map/rpo,rt->pto/dot_general | solution.py:43
  (4 shorter events, 0.0 us)
Async XLA Ops:
  5.5 40.2 %copy-start = (bf16[512,512]{1,0:T(8,128)(2,1)S(1)}, bf16[512,512]{1,0:T(8,128)(2,1)}, u32[]{:S(2)}) copy-start(bf16[512,512]{1,0:T(8,128)(2,1)} %param.7) | copy-start | bytes 1572868
  5.5 22.9 %all-to-all-start = ((bf16[32,2,4096]{2,1,0:T(2,128)(2,1)}), bf16[32,2,4096]{2,1,0:T(2,128)(2,1)S(1)}, u32[]{:S(2)}, u32[]{:S(2)}) async-start(bf16[32,2,4096]{2,1,0:T(2,128)(2,1)} %copy.15), calls=%async_computation | async-start | bytes 1048576 | tf_op jit(solution)/shard_map/all_to_all | solution.py:24
  28.4 13.7 %all-to-all-start.2 = ((bf16[2,64,2048]{2,0,1:T(2,128)(2,1)}), bf16[2,64,2048]{2,0,1:T(2,128)(2,1)S(1)}, u32[]{:S(2)}, u32[]{:S(2)}) async-start(bf16[2,64,2048]{2,0,1:T(2,128)(2,1)} %copy.25), calls=%async_computation.2 | async-start | bytes 1048576 | tf_op jit(solution)/shard_map/all_to_all | solution.py:26
  42.1 29.8 %all-to-all-start.1 = ((bf16[32,8,2048]{2,1,0:T(8,128)(2,1)}), bf16[32,8,2048]{2,1,0:T(8,128)(2,1)}, u32[]{:S(2)}, u32[]{:S(2)}) async-start(bf16[32,8,2048]{2,1,0:T(8,128)(2,1)} %bitcast_multiply_fusion), calls=%async_computation.1 | async-start | bytes 2097152 | tf_op jit(solution)/shard_map/all_to_all | solution.py:40
where the time goes:
time: 75.8 us; the launch traced here: 75.2 us
  waiting for transfers between devices  29.6 us (39%)
  starting transfers between devices  14.4 us (19%)
  matrix products  13.3 us (18%)
  local copies, waits for them, and re-layouts  11.8 us (16%)
  between operations  3.27 us (4%)
  other arithmetic  2.74 us (4%)
    all_to_all x1, waiting for transfers between devices, per_device(): received = lax.all_to_all(outgoing, ('pair', 'virt'), 0, 0, tiled=True)  22.2 us
    dot_general x1, matrix products, per_device(): product = jnp.dot(chosen, integrals[0], preferred_element_type=jnp.float32)  8.79 us
    all_to_all x1, waiting for transfers between devices, per_device(): chosen = lax.all_to_all(picked, ('pair', 'virt'), 0, 0, tiled=True)  7.37 us
    all_to_all x1, starting transfers between devices, per_device(): chosen = lax.all_to_all(picked, ('pair', 'virt'), 0, 0, tiled=True)  7.33 us
    all_to_all x1, starting transfers between devices, per_device(): received = lax.all_to_all(outgoing, ('pair', 'virt'), 0, 0, tiled=True)  3.62 us
    all_to_all x1, starting transfers between devices, per_device(): lax.all_to_all(amps_pm[:, :, :out_cols], 'virt', split_axis=1, concat_axi...  3.47 us
    dot_general x1, matrix products, per_device(): jnp.einsum('rpo,rt->pto', received, one_hot, preferred_element_type=jnp.f...  3.24 us
    gather x1, local copies, waits for them, and re-layouts, per_device(): picked = jnp.take(amps_pm, tin_all, axis=1)  2.59 us
  transfers between devices with their start and end apart: 3, of which 2 were waited for; matrix products, arithmetic and copies ran while one was open for 25% of the time, Pallas kernels for 0%

commit v1 on v0

--- a/solution.py
+++ b/solution.py
@@ -23,7 +23,15 @@
     picked = jnp.transpose(picked, (1, 0, 2))
     chosen = lax.all_to_all(picked, ("pair", "virt"), 0, 0, tiled=True)
     chosen = chosen.reshape(n_dev * pm_rows, tile_len)
-    sub = lax.all_to_all(amps_pm[:, :, :out_cols], "virt", split_axis=1, concat_axis=0, tiled=True)
+    sub = jnp.concatenate(
+        lax.all_to_all(
+            jnp.stack(jnp.split(amps_pm[:, :, :out_cols], lax.axis_size("virt"), axis=1)),
+            "virt",
+            0,
+            0,
+        ),
+        axis=0,
+    )
     sub = sub.reshape(p_grp, slab // NVT, NVT, AS, TILE)
     fock_four = fock_vv.reshape(NVT, TILE, NVT, TILE)
     onebody = jnp.einsum(

time: 75.8 us -> 74.5 us (0.983)
  waiting for transfers between devices: 29.6 us -> 24.3 us
  local copies, waits for them, and re-layouts: 11.8 us -> 13.7 us
  matrix products: 13.3 us -> 14.7 us
  other arithmetic: 2.74 us -> 3.56 us
    all_to_all x1, waiting for transfers between devices: 22.2 us -> 16.5 us  [per_device(): received = lax.all_to_all(outgoing, ('pair', 'virt'), 0, 0, tiled=True)]
    another operation x0 -> x2, local copies, waits for them, and re-layouts: none -> 3.19 us  [the longest x1 2.05 us: per_device(): sub = sub.reshape(p_grp, slab // NVT, NVT, AS, TILE)]
    dot_general x1, matrix products: 1.27 us -> 3.84 us  [per_device(): jnp.einsum('pkqsd,bjqd->pkbsj', sub, fock_four, preferred_element_type=jn...]
    reshape x1, local copies, waits for them, and re-layouts: 0.65 us -> 2.08 us  [per_device(): onebody = jnp.einsum('pkqsd,bjqd->pkbsj', sub, fock_four, preferred_eleme...]
    unnamed x3 -> x0, local copies, waits for them, and re-layouts: 1.34 us -> none
    dot_general x1, matrix products: 3.24 us -> 2.02 us  [per_device(): jnp.einsum('rpo,rt->pto', received, one_hot, preferred_element_type=jnp.f...]
    reshape x1, local copies, waits for them, and re-layouts: 0.53 us -> 1.65 us  [per_device(): fock_four = fock_vv.reshape(NVT, TILE, NVT, TILE)]
    slice x1 -> x0, local copies, waits for them, and re-layouts: 1.08 us -> none  [per_device(): amps_pm[:, :, :out_cols]]
  transfers between devices with their start and end apart: 3 -> 3, of which waited for: 2 -> 2; matrix products, arithmetic and copies ran while one was open for 25% -> 33% of each run, Pallas kernels for 0% -> 0%
where the time goes in v1:
time: 74.5 us; the launch traced here: 73.8 us
  waiting for transfers between devices  24.3 us (33%)
  matrix products  14.7 us (20%)
  starting transfers between devices  14.3 us (19%)
  local copies, waits for them, and re-layouts  13.7 us (18%)
  other arithmetic  3.56 us (5%)
  between operations  3.36 us (5%)
    all_to_all x1, waiting for transfers between devices, per_device(): received = lax.all_to_all(outgoing, ('pair', 'virt'), 0, 0, tiled=True)  16.5 us
    dot_general x1, matrix products, per_device(): product = jnp.dot(chosen, integrals[0], preferred_element_type=jnp.float32)  8.79 us
    all_to_all x1, waiting for transfers between devices, per_device(): chosen = lax.all_to_all(picked, ('pair', 'virt'), 0, 0, tiled=True)  7.72 us
    all_to_all x1, starting transfers between devices, per_device(): chosen = lax.all_to_all(picked, ('pair', 'virt'), 0, 0, tiled=True)  7.33 us
    dot_general x1, matrix products, per_device(): jnp.einsum('pkqsd,bjqd->pkbsj', sub, fock_four, preferred_element_type=jn...  3.84 us
    all_to_all x1, starting transfers between devices, per_device(): received = lax.all_to_all(outgoing, ('pair', 'virt'), 0, 0, tiled=True)  3.49 us
    all_to_all x1, starting transfers between devices, per_device(): lax.all_to_all(jnp.stack(jnp.split(amps_pm[:, :, :out_cols], lax.axis_siz...  3.47 us
    gather x1, local copies, waits for them, and re-layouts, per_device(): picked = jnp.take(amps_pm, tin_all, axis=1)  2.59 us
  transfers between devices with their start and end apart: 3, of which 2 were waited for; matrix products, arithmetic and copies ran while one was open for 33% of the time, Pallas kernels for 0%

profile of v1, /device:TPU:0, one launch (start us, length us, event | category | flops | bytes accessed | tf_op | source)
XLA Modules:
  0.0 73.8 jit_solution(8951630119658892802)
XLA Ops:
  0.0 0.8 %slice_bitcast_fusion.4 = (s32[32]{0:T(128)S(1)}, s32[32]{0:T(128)S(1)}) fusion(s32[32,2]{0,1:T(2,128)} %param.8), kind=kLoop, calls=%fused_computation.29 | loop fusion | flops 96 | bytes 512 | tf_op jit(solution)/shard_map/eq | solution.py:50
  0.8 0.7 and_bitcast_fusion
  1.5 2.6 %gather_fusion = bf16[32,2,4096]{2,0,1:T(8,128)(2,1)S(1)} fusion(bf16[2,64,4096]{2,1,0:T(8,128)(2,1)} %param.5, s32[1024]{0:T(1024)S(1)} %pad_clamp_fusion), kind=kCustom, calls=%fused_computation | custom fusion | bytes 1048704 | tf_op jit(solution)/shard_map/jit(_take)/gather | solution.py:22
  4.0 0.1 broadcast_select_fusion
  4.2 1.3 %copy.11 = bf16[32,2,4096]{2,1,0:T(2,128)(2,1)} copy(bf16[32,2,4096]{2,0,1:T(8,128)(2,1)S(1)} %broadcast_select_fusion) | data formatting | bytes 1048576 | tf_op jit(solution)/shard_map/jit(_take)/select_n | solution.py:22
  5.5 7.3 %all-to-all-start = ((bf16[32,2,4096]{2,1,0:T(2,128)(2,1)}), bf16[32,2,4096]{2,1,0:T(2,128)(2,1)S(1)}, u32[]{:S(2)}, u32[]{:S(2)}) async-start(bf16[32,2,4096]{2,1,0:T(2,128)(2,1)} %copy.11), calls=%async_computation | async-start | bytes 1048576 | tf_op jit(solution)/shard_map/all_to_all | solution.py:24
  12.8 0.8 %constant_dynamic-slice_fusion = s32[1,2]{0,1:T(2,128)S(1)} fusion(s32[32,2]{0,1:T(2,128)} %param.8, s32[]{:T(128)S(6)} %select_n.29), kind=kLoop, calls=%fused_computation.30 | loop fusion | bytes 20 | tf_op jit(solution)/shard_map/jit(dynamic_index_in_dim)/dynamic_slice | solution.py:40
  13.6 0.5 slice.17
  16.7 0.1 mul.42
  16.8 1.2 %dynamic_slice.8 = s32[1]{0:T(128)} dynamic-slice(s32[32]{0:T(128)} %param.9, s32[]{:T(128)S(6)} %select_n.29), dynamic_slice_sizes={1} | dynamic-slice | bytes 12 | tf_op jit(solution)/shard_map/jit(dynamic_index_in_dim)/dynamic_slice | solution.py:41
  18.7 1.1 %slice_bitcast_fusion.3 = (bf16[1,2,16,2048]{3,2,1,0:T(8,128)(2,1)S(1)}, bf16[1,2,16,2048]{3,2,1,0:T(8,128)(2,1)S(1)}, bf16[1,2,16,2048]{3,2,1,0:T(8,128)(2,1)S(1)}, bf16[1,2,16,2048]{3,2,1,0:T(8,128)(2,1)S(1)}) fusion(bf16[2,64,4096]{2,1,0:T(8,128)(2,1)} %param.5), kind=kLoop, calls=%fused_computation.19 | loop fusion | bytes 1048576 | tf_op jit(solution)/shard_map/stack | solution.py:28
  19.9 0.9 %pad_maximum_fusion = bf16[4,2,16,2048]{3,2,1,0:T(8,128)(2,1)} fusion(bf16[1,2,16,2048]{3,2,1,0:T(8,128)(2,1)S(1)} %get-tuple-element.7, bf16[1,2,16,2048]{3,2,1,0:T(8,128)(2,1)S(1)} %get-tuple-element.8, bf16[1,2,16,2048]{3,2,1,0:T(8,128)(2,1)S(1)} %get-tuple-element.6, bf16[1,2,16,2048]{3,2,1,0:T(8,128)(2,1)S(1)} %get-tuple-element.5), kind=kLoop, calls=%fused_computation.14 | loop fusion | flops 786432 | bytes 1048576 | tf_op jit(solution)/shard_map/stack | solution.py:28
  20.7 7.7 %all-to-all-done = bf16[32,2,4096]{2,1,0:T(2,128)(2,1)S(1)} async-done(((bf16[32,2,4096]{2,1,0:T(2,128)(2,1)}), bf16[32,2,4096]{2,1,0:T(2,128)(2,1)S(1)}, u32[]{:S(2)}, u32[]{:S(2)}) %all-to-all-start) | async-done | bytes 524320 | tf_op jit(solution)/shard_map/all_to_all | solution.py:24
  28.4 3.5 %all-to-all-start.2 = ((bf16[4,2,16,2048]{3,2,1,0:T(8,128)(2,1)}), bf16[4,2,16,2048]{3,2,1,0:T(8,128)(2,1)S(1)}, u32[]{:S(2)}, u32[]{:S(2)}) async-start(bf16[4,2,16,2048]{3,2,1,0:T(8,128)(2,1)} %pad_maximum_fusion), calls=%async_computation.2 | async-start | bytes 1048576 | tf_op jit(solution)/shard_map/all_to_all | solution.py:27
  31.9 0.2 reshape.30
  32.1 8.8 %fusion.10 = bf16[8,8,2048]{2,1,0:T(8,128)(2,1)S(1)} fusion(bf16[64,4096]{1,0:T(8,128)(2,1)S(1)} %reshape.30, bf16[1,4096,2048]{2,1,0:T(8,128)(2,1)} %param.6, f32[]{:T(128)} %bitcast.5), kind=kOutput, calls=%fused_computation.8 | convolution fusion | flops 1074003968 | bytes 17563652 | tf_op jit(solution)/shard_map/dot_general | solution.py:42
  40.9 1.1 %bitcast_multiply_fusion = bf16[32,8,2048]{2,1,0:T(8,128)(2,1)} fusion(bf16[32]{0:T(256)(128)(2,1)S(1)} %mul.42, bf16[8,8,2048]{2,1,0:T(8,128)(2,1)S(1)} %fusion.10), kind=kLoop, calls=%fused_computation.12 | loop fusion | flops 524288 | bytes 1310784 | tf_op jit(solution)/shard_map/mul | solution.py:46
  42.1 0.0 all-to-all-done.2
  42.1 3.5 %all-to-all-start.1 = ((bf16[32,8,2048]{2,1,0:T(8,128)(2,1)}), bf16[32,8,2048]{2,1,0:T(8,128)(2,1)S(1)}, u32[]{:S(2)}, u32[]{:S(2)}) async-start(bf16[32,8,2048]{2,1,0:T(8,128)(2,1)} %bitcast_multiply_fusion), calls=%async_computation.1 | async-start | bytes 2097152 | tf_op jit(solution)/shard_map/all_to_all | solution.py:48
  45.6 1.6 %reshape.31 = bf16[8,64,8,64]{3,2,1,0:T(8,128)(2,1)S(1)} reshape(bf16[512,512]{1,0:T(8,128)(2,1)} %param.7) | data formatting | bytes 1048576 | tf_op jit(solution)/shard_map/reshape | solution.py:36
  47.2 2.1 %reshape.42 = bf16[8,2,8,32,64,1]{4,3,2,1,0,5:T(8,128)(2,1)} reshape(bf16[4,2,16,2048]{3,2,1,0:T(8,128)(2,1)S(1)} %all-to-all-done.2) | data formatting | bytes 1048576 | tf_op jit(solution)/shard_map/reshape;reshape | solution.py:35
  49.3 3.8 %convolution_bitcast_fusion.1 = f32[8,2,8,32,64]{4,3,2,1,0:T(8,128)} fusion(bf16[8,64,8,64,1,1]{3,2,1,0,5,4:T(8,128)(2,1)S(1)} %bitcast.52, bf16[8,2,8,32,64,1]{4,3,2,1,0,5:T(8,128)(2,1)} %reshape.42), kind=kOutput, calls=%fused_computation.9 | convolution fusion | flops 268435456 | bytes 2097152 | tf_op jit(solution)/shard_map/pkqsd,bjqd->pkbsj/dot_general | solution.py:37
  53.1 2.1 %reshape.32 = f32[8,16,2048]{2,1,0:T(8,128)S(1)} reshape(f32[8,2,8,32,64]{4,3,2,1,0:T(8,128)} %convolution_bitcast_fusion.1) | data formatting | bytes 2097152 | tf_op jit(solution)/shard_map/reshape | solution.py:39
  55.2 16.5 %all-to-all-done.1 = bf16[32,8,2048]{2,1,0:T(8,128)(2,1)S(1)} async-done(((bf16[32,8,2048]{2,1,0:T(8,128)(2,1)}), bf16[32,8,2048]{2,1,0:T(8,128)(2,1)S(1)}, u32[]{:S(2)}, u32[]{:S(2)}) %all-to-all-start.1) | async-done | bytes 1048608 | tf_op jit(solution)/shard_map/all_to_all | solution.py:48
  71.8 2.0 %fusion.3 = bf16[8,16,2048]{2,1,0:T(8,128)(2,1)} fusion(f32[8,16,2048]{2,1,0:T(8,128)S(1)} %reshape.32, bf16[32,8,2048]{2,1,0:T(8,128)(2,1)S(1)} %all-to-all-done.1, s32[32]{0:T(128)S(1)} %get-tuple-element.9, s32[16]{0:T(128)S(1)} %iota_add_fusion), kind=kOutput, calls=%fused_computation.5 | convolution fusion | flops 17302016 | bytes 2621632 | tf_op jit(solution)/shard_map/rpo,rt->pto/dot_general | solution.py:51
  (4 shorter events, 0.0 us)
Async XLA Ops:
  5.5 22.9 %all-to-all-start = ((bf16[32,2,4096]{2,1,0:T(2,128)(2,1)}), bf16[32,2,4096]{2,1,0:T(2,128)(2,1)S(1)}, u32[]{:S(2)}, u32[]{:S(2)}) async-start(bf16[32,2,4096]{2,1,0:T(2,128)(2,1)} %copy.11), calls=%async_computation | async-start | bytes 1048576 | tf_op jit(solution)/shard_map/all_to_all | solution.py:24
  28.4 13.6 %all-to-all-start.2 = ((bf16[4,2,16,2048]{3,2,1,0:T(8,128)(2,1)}), bf16[4,2,16,2048]{3,2,1,0:T(8,128)(2,1)S(1)}, u32[]{:S(2)}, u32[]{:S(2)}) async-start(bf16[4,2,16,2048]{3,2,1,0:T(8,128)(2,1)} %pad_maximum_fusion), calls=%async_computation.2 | async-start | bytes 1048576 | tf_op jit(solution)/shard_map/all_to_all | solution.py:27
  42.1 29.7 %all-to-all-start.1 = ((bf16[32,8,2048]{2,1,0:T(8,128)(2,1)}), bf16[32,8,2048]{2,1,0:T(8,128)(2,1)S(1)}, u32[]{:S(2)}, u32[]{:S(2)}) async-start(bf16[32,8,2048]{2,1,0:T(8,128)(2,1)} %bitcast_multiply_fusion), calls=%async_computation.1 | async-start | bytes 2097152 | tf_op jit(solution)/shard_map/all_to_all | solution.py:48
